TPU v7x, 512 devices: a whole 4x8x8 slice. The times are simulated.
512 devices in a mesh: grp: 32 (over x, y), tp: 16 (over z, core).
Axes of the slice: x: 4, y: 8, z: 8, core: 2. Of those that a mesh axis runs over, the one named last changes fastest.
Arguments:
- patches: bfloat16 [16384, 1664], P('grp'), may hold values from -6 to 6
- patch_image: int32 [16384], P('grp'), may hold values from 0 to 4095, as said below
- vis_gain: float32 [1664], replicated, may hold values from 0.25 to 1.75
- vis_bias: float32 [1664], replicated, may hold values from -3 to 3
- vis_qkv: bfloat16 [3, 1664, 1664], P(None, None, 'tp'), may hold values from -2 to 2
- vis_out: bfloat16 [1664, 1664], P('tp'), may hold values from -0.15625 to 0.15625
- merge_weight: bfloat16 [4, 1664, 1024], P(None, 'tp'), may hold values from -0.078125 to 0.078125
- positions: int32 [4096], P('grp'), may hold values from 0 to 12287, as said below
- text: bfloat16 [8192, 1024], P('grp'), may hold values from -6 to 6
- dec_gain: float32 [1024], replicated, may hold values from 0.25 to 1.75
- dec_bias: float32 [1024], replicated, may hold values from -3 to 3
- dec_qkv: bfloat16 [3, 1024, 1024], P(None, None, 'tp'), may hold values from -2 to 2
Outputs:
- dec_attn: bfloat16 [12288, 1024], P('grp', 'tp')
Inputs may be any that keep to these rules, and one draw needn't show every extreme that they name: `patch_image`: each aligned run of four patches belongs to one image. Groups 2j and 2j+1 are partners: the last image of group 2j continues as the first image of group 2j+1; no other image is shared between groups. All positions are distinct; each group's block of 384 positions holds exactly 128 of them; the 128 merged rows of one group put at most 8 positions into any one group's block.
All inputs are finite; a program needn't handle non-finite values.
Results may differ from a plain program's by a relative error of at most 0.025.
Values may be sent and summed in bfloat16 or wider, within the bound.
No kernel may reach another device: no remote copies, remote signals or barrier semaphores. Data moves between devices by JAX's collectives and lax.ppermute only.
A program may use at most 128 MiB of HBM per device.

v0:
```python
import jax
import jax.numpy as jnp
from jax import lax
from jax.sharding import PartitionSpec as P

HD = 104
DH = 64
layer_eps = 1e-05


def swapped(value, axis, stride):
    return lax.ppermute(value, axis, [(i, i ^ 1 << stride) for i in range(lax.axis_size(axis))])


def normalize(values, gain, bias):
    mean = jnp.mean(values, axis=-1, keepdims=True)
    centred = values - mean
    spread = jnp.mean(centred * centred, axis=-1, keepdims=True)
    return centred * lax.rsqrt(spread + layer_eps) * gain + bias


def body(
    patches,
    patch_image,
    vis_gain,
    vis_bias,
    vis_qkv,
    vis_out,
    merge_weight,
    positions,
    text,
    dec_gain,
    dec_bias,
    dec_qkv,
):
    rows = patches.shape[0]
    heads = vis_qkv.shape[2] // HD
    patches_f = patches.astype(jnp.float32)
    normed = normalize(patches_f, vis_gain, vis_bias).astype(jnp.bfloat16)
    proj = jnp.einsum("pd,sde->spe", normed, vis_qkv, preferred_element_type=jnp.float32).astype(
        jnp.bfloat16
    )
    query = proj[0].reshape(rows, heads, HD)
    partner_kv, partner_ids = swapped((proj[1:], patch_image), "grp", 0)
    both_kv = jnp.concatenate([proj[1:], partner_kv], axis=1)
    both_ids = jnp.concatenate([patch_image, partner_ids], axis=0)
    keys = both_kv[0].reshape(2 * rows, heads, HD)
    values = both_kv[1].reshape(2 * rows, heads, HD)
    scores = jnp.einsum("phe,khe->hpk", query, keys, preferred_element_type=jnp.float32) * HD ** (
        -0.5
    )
    same = patch_image[:, None] == both_ids[None, :]
    top = jnp.max(jnp.where(same, scores, -1e30), axis=2, keepdims=True)
    expo = jnp.where(same, jnp.exp(scores - top), 0.0)
    weights = (expo / jnp.sum(expo, axis=2, keepdims=True)).astype(jnp.bfloat16)
    attended = jnp.einsum(
        "hpk,khe->phe", weights, values, preferred_element_type=jnp.float32
    ).astype(jnp.bfloat16)
    attended = attended.reshape(rows, heads * HD)
    width = patches.shape[1] // lax.axis_size("tp")
    mixed = lax.psum_scatter(
        lax.dot_general(
            vis_out, attended, (((0,), (1,)), ((), ())), preferred_element_type=jnp.float32
        ).astype(jnp.bfloat16),
        "tp",
        scatter_dimension=0,
        tiled=True,
    ).astype(jnp.float32)
    own_cols = lax.dynamic_slice_in_dim(patches_f, lax.axis_index("tp") * width, width, 1)
    visual = (mixed + own_cols.T).astype(jnp.bfloat16)
    windows = visual.reshape(width, rows // 4, 4)
    partial_rows = jnp.einsum(
        "cmk,kce->me", windows, merge_weight, preferred_element_type=jnp.float32
    )
    groups = lax.axis_size("grp")
    here = lax.axis_index("grp")
    merged_count = rows // 4
    text_count = text.shape[0]
    tok = text_count + merged_count
    cap = merged_count // min(groups, 16)
    target = positions // tok
    member = (target[:, None] == jnp.arange(groups, dtype=jnp.int32)[None, :]).astype(jnp.int32)
    rank = jnp.sum(jnp.cumsum(member, axis=0) * member, axis=1) - 1
    slot = target * cap + rank
    select = slot[None, :] == jnp.arange(groups * cap, dtype=jnp.int32)[:, None]
    select_bf = select.astype(jnp.bfloat16)
    bucket_pos = jnp.sum(jnp.where(select, positions[None, :] + 1, 0), axis=1) - 1
    merged = lax.psum(partial_rows.astype(jnp.bfloat16), "tp")
    packed = jnp.dot(select_bf, merged, preferred_element_type=jnp.float32).astype(jnp.bfloat16)
    got_rows, got_pos = (
        lax.all_to_all(packed, "grp", split_axis=0, concat_axis=0, tiled=True),
        lax.all_to_all(bucket_pos, "grp", split_axis=0, concat_axis=0, tiled=True),
    )
    local_pos = got_pos - here * tok
    place = jnp.arange(tok, dtype=jnp.int32)
    landing = (local_pos[None, :] == place[:, None]) & (got_pos[None, :] >= 0)
    image_here = jnp.any(landing, axis=1).astype(jnp.int32)
    text_index = place - (jnp.cumsum(image_here) - image_here)
    text_pick = (image_here[:, None] == 0) & (
        text_index[:, None] == jnp.arange(text_count, dtype=jnp.int32)[None, :]
    )
    prompt = jnp.dot(landing.astype(jnp.bfloat16), got_rows, preferred_element_type=jnp.float32)
    prompt = prompt + jnp.dot(
        text_pick.astype(jnp.bfloat16), text, preferred_element_type=jnp.float32
    )
    dnorm = normalize(prompt, dec_gain, dec_bias).astype(jnp.bfloat16)
    dproj = jnp.einsum("td,sde->ste", dnorm, dec_qkv, preferred_element_type=jnp.float32).astype(
        jnp.bfloat16
    )
    dheads = dec_qkv.shape[2] // DH
    dquery = dproj[0].reshape(tok, dheads, DH)
    query_pos = here * tok + place
    best = jnp.full((dheads, tok), -1e30, jnp.float32)
    key_rows = lax.all_gather(dproj[1], "grp", axis=0, tiled=True).reshape(-1, dheads, DH)
    value_rows = lax.all_gather(dproj[2], "grp", axis=0, tiled=True).reshape(-1, dheads, DH)
    key_pos = jnp.arange(key_rows.shape[0], dtype=jnp.int32)
    score = jnp.einsum(
        "the,rhe->htr", dquery, key_rows, preferred_element_type=jnp.float32
    ) * DH ** (-0.5)
    allowed = key_pos[None, :] <= query_pos[:, None]
    new_best = jnp.maximum(best, jnp.max(jnp.where(allowed[None], score, -1e30), axis=2))
    expo_d = jnp.where(allowed[None], jnp.exp(score - new_best[:, :, None]), 0.0)
    total = jnp.sum(expo_d, axis=2)
    acc = jnp.einsum(
        "htr,rhe->hte", expo_d.astype(jnp.bfloat16), value_rows, preferred_element_type=jnp.float32
    )
    best, total, acc = (new_best, total, acc)
    result = acc / total[:, :, None]
    return result.transpose(1, 0, 2).reshape(tok, dheads * DH).astype(jnp.bfloat16)


def solution(mesh):
    in_specs = (
        P("grp", None),
        P("grp"),
        P(),
        P(),
        P(None, None, "tp"),
        P("tp", None),
        P(None, "tp", None),
        P("grp"),
        P("grp", None),
        P(),
        P(),
        P(None, None, "tp"),
    )
    out_specs = P("grp", "tp")
    return jax.shard_map(body, mesh=mesh, in_specs=in_specs, out_specs=out_specs, check_vma=False)
```

profile of v0, /device:TPU:8, one launch (start us, length us, event | category | flops | bytes accessed | tf_op | source)
XLA Modules:
  0.0 415.6 jit_solution(2915710087922539153)
XLA Ops:
  6.5 0.0 copy-start
  6.5 0.0 reduce-scatter.4.cloned.1.call-start
  6.6 1.9 convert_reduce_fusion
  8.5 0.1 copy-done.1
  8.6 0.6 multiply_reduce_fusion
  9.2 0.0 copy-start.4
  9.2 1.0 fusion.6
  10.3 7.7 %collective-permute-start = (bf16[2,512,104]{1,2,0:T(8,128)(2,1)S(1)}, bf16[2,512,104]{1,2,0:T(8,128)(2,1)S(1)}, u32[]{:S(2)}, u32[]{:S(2)}) collective-permute-start(bf16[2,512,104]{1,2,0:T(8,128)(2,1)S(1)} %slice.38), channel_id=1, source_target_pairs={{0,16},{16,0},{32,48},{48,32},{64,80},{80,64},{96,112},{112,96},{1... | collective-permute-start | bytes 638984 | tf_op jit(solution)/shard_map/ppermute | solution.py:12
  18.1 1.9 collective-permute-start.1
  20.0 3.6 collective-permute-done.1
  23.6 0.0 collective-permute-done
  23.6 0.6 fusion.5
  24.2 1.4 copy-done.2
  25.5 0.7 fusion.13
  26.2 4.3 %fusion.4 = bf16[1664,512]{0,1:T(8,128)(2,1)} fusion(bf16[104,1664]{1,0:T(8,128)(2,1)S(1)} %copy-done.6, f32[512,1024]{1,0:T(8,128)} %copy-done.2, f32[512]{0:T(512)S(1)} %fusion.13, f32[512]{0:T(512)S(1)} %get-tuple-element.11, s32[1024]{0:T(1024)S(1)} %pad_add_fusion, s32[512]{0:T(512)S(1)} %copy-done.4, bf16[2,512,104]{1,2,0:T(8,128)(2,1)S(1)} %slice.38, ...), kind=kOutput, calls=%fused_computation.10 | convolution fusion | flops 290738176 | bytes 4583424 | tf_op jit(solution)/shard_map/dot_general | solution.py:62
  30.5 3.6 copy.17
  34.1 0.0 reduce-scatter.4.cloned.1.call-update
  34.1 0.0 all-reduce.2.cloned.1.call-start
  34.2 0.0 copy-start.11
  34.2 2.0 convert_element_type.82
  36.2 0.0 copy-done.11
  36.2 0.1 fusion.64
  36.3 0.2 reduce_window_sum.30
  36.4 0.2 select_reduce_fusion.2
  36.6 0.1 select_reduce_fusion.1
  36.8 59.7 %reduce-scatter.4.cloned.1.call-done = bf16[104,512]{1,0:T(8,128)(2,1)} async-done(((bf16[1664,512]{1,0:T(8,128)(2,1)}), bf16[104,512]{1,0:T(8,128)(2,1)}) %reduce-scatter.4.cloned.1.call-update) | async-done | bytes 106512
  96.5 1.0 copy.18
  97.5 1.2 fusion.49
  98.7 2.2 fusion.15
  100.9 0.0 all-reduce.2.cloned.1.call-update
  100.9 0.0 copy-start.3
  100.9 0.7 sub.80
  101.6 9.9 %all-to-all-start = ((s32[32,8,1]{1,2,0:T(1,128)}), s32[32,8,1]{1,2,0:T(1,128)S(1)}, u32[]{:S(2)}, u32[]{:S(2)}) async-start(s32[32,8,1]{1,2,0:T(1,128)} %bitcast), calls=%async_computation | async-start | bytes 32768 | tf_op jit(solution)/shard_map/all_to_all | solution.py:92
  111.5 102.0 %all-reduce.2.cloned.1.call-done = bf16[128,1024]{1,0:T(8,128)(2,1)} async-done(((bf16[128,1024]{1,0:T(8,128)(2,1)}), bf16[128,1024]{1,0:T(8,128)(2,1)}) %all-reduce.2.cloned.1.call-update) | async-done | bytes 262160 | tf_op jit(solution)/shard_map/psum | solution.py:88
  213.5 2.0 fusion.14
  215.5 0.0 all-to-all-done
  215.5 9.8 %all-to-all-start.1 = ((bf16[32,8,1024]{2,1,0:T(8,128)(2,1)}), bf16[32,8,1024]{2,1,0:T(8,128)(2,1)S(1)}, u32[]{:S(2)}, u32[]{:S(2)}) async-start(bf16[32,8,1024]{2,1,0:T(8,128)(2,1)} %fusion.14), calls=%async_computation.1 | async-start | bytes 1048576 | tf_op jit(solution)/shard_map/all_to_all | solution.py:91
  225.4 0.0 all-gather.5.cloned.1.call-start
  225.5 0.1 sub.83
  225.6 0.1 compare_reduce_fusion
  225.6 0.1 ge.16
  225.7 0.2 fusion.45
  225.9 0.3 reduce-window.9
  226.2 0.1 slice.33
  226.3 0.1 slice_reduce_fusion
  226.4 0.1 fusion.65
  226.5 16.5 %all-to-all-done.1 = bf16[32,8,1024]{2,1,0:T(8,128)(2,1)S(1)} async-done(((bf16[32,8,1024]{2,1,0:T(8,128)(2,1)}), bf16[32,8,1024]{2,1,0:T(8,128)(2,1)S(1)}, u32[]{:S(2)}, u32[]{:S(2)}) %all-to-all-start.1) | async-done | bytes 524320 | tf_op jit(solution)/shard_map/all_to_all | solution.py:91
  243.0 0.4 fusion.42
  243.4 0.0 copy-start.5
  243.4 0.0 copy-start.9
  243.4 0.0 copy-start.10
  243.4 0.5 fusion.75
  244.0 0.3 multiply_reduce_fusion.1
  244.3 0.1 copy-done.5
  244.4 0.5 fusion.37
  245.0 0.6 fusion.74
  245.6 0.0 all-gather.5.cloned.1.call-update
  245.7 0.2 all-gather.7.cloned.1.call-start
  245.9 0.3 all-gather.7.cloned.1.call-update
  246.3 71.2 %all-gather.5.cloned.1.call-done = bf16[1,12288,64]{1,2,0:T(8,128)(2,1)} async-done(((bf16[1,384,64]{1,2,0:T(8,128)(2,1)}), bf16[1,12288,64]{1,2,0:T(8,128)(2,1)}) %all-gather.5.cloned.1.call-update) | async-done | bytes 1572880 | tf_op jit(solution)/shard_map/all_gather | solution.py:114
  317.4 9.3 %select_reduce_fusion = (f32[384]{0:T(512)S(1)}, f32[384,12288]{1,0:T(8,128)}) fusion(s32[384]{0:T(512)S(1)} %iota_add_fusion, bf16[1,12288,64]{1,2,0:T(8,128)(2,1)} %all-gather.5.cloned.1.call-done, bf16[3,384,64]{1,2,0:T(8,128)(2,1)S(1)} %convert_bitcast_fusion.1), kind=kOutput, calls=%fused_computation.1 | convolution fusion | flops 622853760 | bytes 20499968 | tf_op jit(solution)/shard_map/the,rhe->htr/dot_general | solution.py:117
  326.7 11.1 %fusion = f32[384]{0:T(512)S(1)} fusion(f32[384,12288]{1,0:T(8,128)} %get-tuple-element.16, f32[384]{0:T(512)S(1)} %broadcast_maximum_fusion, s32[384]{0:T(512)S(1)} %iota_add_fusion), kind=kLoop, calls=%fused_computation.4 | loop fusion | flops 18873984 | bytes 18878976 | tf_op jit(solution)/shard_map/reduce_sum | solution.py:123
  337.8 60.2 %all-gather.7.cloned.1.call-done = bf16[1,12288,64]{1,2,0:T(8,128)(2,1)} async-done(((bf16[1,384,64]{1,2,0:T(8,128)(2,1)}), bf16[1,12288,64]{1,2,0:T(8,128)(2,1)}) %all-gather.7.cloned.1.call-update) | async-done | bytes 1572880 | tf_op jit(solution)/shard_map/all_gather | solution.py:115
  398.0 11.1 %fusion.22 = bf16[384,64]{0,1:T(8,128)(2,1)} fusion(bf16[1,12288,64]{1,2,0:T(8,128)(2,1)} %all-gather.7.cloned.1.call-done, f32[384,12288]{1,0:T(8,128)} %get-tuple-element.16, f32[384]{0:T(512)S(1)} %broadcast_maximum_fusion, s32[384]{0:T(512)S(1)} %iota_add_fusion, f32[384]{0:T(512)S(1)} %fusion), kind=kOutput, calls=%fused_computation.34 | convolution fusion | flops 622903296 | bytes 20500992 | tf_op jit(solution)/shard_map/htr,rhe->hte/dot_general | solution.py:124
  (29 shorter events, 0.3 us)
Async XLA Ops:
  6.5 2.6 copy-start
  6.5 2.1 copy-start.1
  6.5 2.7 copy-start.8
  6.5 2.7 copy-start.7
  6.5 89.9 %reduce-scatter.4.cloned.1.call-start = ((), (), s32[]{:S(2)}) async-start(), calls=%async_computation.6 | async-start | bytes 1810432
  9.2 8.9 %copy-start.4 = (s32[512]{0:T(512)S(1)}, s32[512]{0:T(512)}, u32[]{:S(2)}) copy-start(s32[512]{0:T(512)} %param.13) | copy-start | bytes 6148
  10.3 13.2 %collective-permute-start = (bf16[2,512,104]{1,2,0:T(8,128)(2,1)S(1)}, bf16[2,512,104]{1,2,0:T(8,128)(2,1)S(1)}, u32[]{:S(2)}, u32[]{:S(2)}) collective-permute-start(bf16[2,512,104]{1,2,0:T(8,128)(2,1)S(1)} %slice.38), channel_id=1, source_target_pairs={{0,16},{16,0},{32,48},{48,32},{64,80},{80,64},{96,112},{112,96},{1... | collective-permute-start | bytes 638984 | tf_op jit(solution)/shard_map/ppermute | solution.py:12
  18.1 5.5 %collective-permute-start.1 = (s32[512]{0:T(512)S(1)}, s32[512]{0:T(512)S(1)}, u32[]{:S(2)}, u32[]{:S(2)}) collective-permute-start(s32[512]{0:T(512)S(1)} %copy-done.4), channel_id=1, source_target_pairs={{0,16},{16,0},{32,48},{48,32},{64,80},{80,64},{96,112},{112,96},{1... | collective-permute-start | bytes 6152 | tf_op jit(solution)/shard_map/ppermute | solution.py:12
  23.6 2.6 copy-start.6
  24.2 1.4 copy-start.2
  34.1 179.3 %all-reduce.2.cloned.1.call-start = ((), (), s32[]{:S(2)}) async-start(), calls=%async_computation.3 | async-start | bytes 524288 | tf_op jit(solution)/shard_map/psum | solution.py:88
  34.2 2.0 copy-start.11
  100.9 142.5 %copy-start.3 = (bf16[256,1024]{1,0:T(8,128)(2,1)S(1)}, bf16[256,1024]{1,0:T(8,128)(2,1)}, u32[]{:S(2)}) copy-start(bf16[256,1024]{1,0:T(8,128)(2,1)} %param.20) | copy-start | bytes 1572868
  101.6 113.9 %all-to-all-start = ((s32[32,8,1]{1,2,0:T(1,128)}), s32[32,8,1]{1,2,0:T(1,128)S(1)}, u32[]{:S(2)}, u32[]{:S(2)}) async-start(s32[32,8,1]{1,2,0:T(1,128)} %bitcast), calls=%async_computation | async-start | bytes 32768 | tf_op jit(solution)/shard_map/all_to_all | solution.py:92
  215.5 27.5 %all-to-all-start.1 = ((bf16[32,8,1024]{2,1,0:T(8,128)(2,1)}), bf16[32,8,1024]{2,1,0:T(8,128)(2,1)S(1)}, u32[]{:S(2)}, u32[]{:S(2)}) async-start(bf16[32,8,1024]{2,1,0:T(8,128)(2,1)} %fusion.14), calls=%async_computation.1 | async-start | bytes 1048576 | tf_op jit(solution)/shard_map/all_to_all | solution.py:91
  225.4 92.1 %all-gather.5.cloned.1.call-start = ((), (), s32[]{:S(2)}) async-start(), calls=%async_computation.4 | async-start | bytes 1622016 | tf_op jit(solution)/shard_map/all_gather | solution.py:114
  243.4 1.0 copy-start.5
  243.4 1.0 copy-start.9
  243.4 1.0 copy-start.10
  245.7 152.3 %all-gather.7.cloned.1.call-start = ((), (), s32[]{:S(2)}) async-start(), calls=%async_computation.5 | async-start | bytes 1622016 | tf_op jit(solution)/shard_map/all_gather | solution.py:115
Sparse Core Ops, SparseCore 0:
  34.3 62.1 reduce-scatter.3
  101.0 112.4 all-reduce.1
  245.8 71.5 all-gather.4
  320.4 77.5 all-gather.6
where the time goes:
time: 416 us
  waiting for transfers between devices  313 us (75%)
  matrix products  32 us (8%)
  starting transfers between devices  29.7 us (7%)
  other arithmetic  19 us (5%)
  between operations  13.4 us (3%)
  local copies, waits for them, and re-layouts  8.01 us (2%)
    psum x1, waiting for transfers between devices, body(): merged = lax.psum(partial_rows.astype(jnp.bfloat16), 'tp')  102 us
    all_gather x1, waiting for transfers between devices, body(): lax.all_gather(dproj[1], 'grp', axis=0, tiled=True).reshape(-1, dheads, DH)  71.2 us
    all_gather x1, waiting for transfers between devices, body(): lax.all_gather(dproj[2], 'grp', axis=0, tiled=True).reshape(-1, dheads, DH)  60.2 us
    unnamed x5, waiting for transfers between devices  60.1 us
    all_to_all x1, waiting for transfers between devices, body(): lax.all_to_all(packed, 'grp', split_axis=0, concat_axis=0, tiled=True)  16.5 us
    dot_general x1, matrix products, body(): jnp.einsum('htr,rhe->hte', expo_d.astype(jnp.bfloat16), value_rows, prefe...  11.1 us
    reduce_sum x1, other arithmetic, body(): total = jnp.sum(expo_d, axis=2)  11.1 us
    all_to_all x1, starting transfers between devices, body(): lax.all_to_all(bucket_pos, 'grp', split_axis=0, concat_axis=0, tiled=True)  9.88 us
  transfers between devices with their start and end apart: 8, of which 6 were waited for; matrix products, arithmetic and copies ran while one was open for 6% of the time, Pallas kernels for 0%

commit v1 on v0

--- a/solution.py
+++ b/solution.py
@@ -85,7 +85,7 @@
     select = slot[None, :] == jnp.arange(groups * cap, dtype=jnp.int32)[:, None]
     select_bf = select.astype(jnp.bfloat16)
     bucket_pos = jnp.sum(jnp.where(select, positions[None, :] + 1, 0), axis=1) - 1
-    merged = lax.psum(partial_rows.astype(jnp.bfloat16), "tp")
+    merged = lax.all_gather(partial_rows.astype(jnp.bfloat16), axis_name="tp").sum(axis=0)
     packed = jnp.dot(select_bf, merged, preferred_element_type=jnp.float32).astype(jnp.bfloat16)
     got_rows, got_pos = (
         lax.all_to_all(packed, "grp", split_axis=0, concat_axis=0, tiled=True),

time: 416 us -> 350 us (0.84)
  waiting for transfers between devices: 313 us -> 245 us
    psum x1 -> x0, waiting for transfers between devices: 102 us -> none  [body(): merged = lax.psum(partial_rows.astype(jnp.bfloat16), 'tp')]
    all_gather x0 -> x1, waiting for transfers between devices: none -> 32.5 us  [body(): lax.all_gather(partial_rows.astype(jnp.bfloat16), axis_name='tp')]
  transfers between devices with their start and end apart: 8 -> 8, of which waited for: 6 -> 6; matrix products, arithmetic and copies ran while one was open for 6% -> 8% of each run, Pallas kernels for 0% -> 0%
where the time goes in v1:
time: 350 us; the launch traced here: 349 us
  waiting for transfers between devices  245 us (70%)
  matrix products  31 us (9%)
  starting transfers between devices  29.7 us (8%)
  other arithmetic  22.2 us (6%)
  between operations  13.4 us (4%)
  local copies, waits for them, and re-layouts  8.01 us (2%)
    all_gather x1, waiting for transfers between devices, body(): lax.all_gather(dproj[1], 'grp', axis=0, tiled=True).reshape(-1, dheads, DH)  70.8 us
    unnamed x5, waiting for transfers between devices  60.7 us
    all_gather x1, waiting for transfers between devices, body(): lax.all_gather(dproj[2], 'grp', axis=0, tiled=True).reshape(-1, dheads, DH)  60.6 us
    all_gather x1, waiting for transfers between devices, body(): lax.all_gather(partial_rows.astype(jnp.bfloat16), axis_name='tp')  32.5 us
    all_to_all x1, waiting for transfers between devices, body(): lax.all_to_all(packed, 'grp', split_axis=0, concat_axis=0, tiled=True)  16.9 us
    dot_general x1, matrix products, body(): jnp.einsum('htr,rhe->hte', expo_d.astype(jnp.bfloat16), value_rows, prefe...  11.1 us
    reduce_sum x1, other arithmetic, body(): total = jnp.sum(expo_d, axis=2)  11.1 us
    all_to_all x1, starting transfers between devices, body(): lax.all_to_all(bucket_pos, 'grp', split_axis=0, concat_axis=0, tiled=True)  9.88 us
  transfers between devices with their start and end apart: 8, of which 6 were waited for; matrix products, arithmetic and copies ran while one was open for 8% of the time, Pallas kernels for 0%

profile of v1, /device:TPU:8, one launch (start us, length us, event | category | flops | bytes accessed | tf_op | source)
XLA Modules:
  0.0 349.4 jit_solution(18053819068211594260)
XLA Ops:
  6.5 0.0 reduce-scatter.4.cloned.1.call-start
  6.6 1.9 convert_reduce_fusion
  8.5 0.1 copy-done.1
  8.6 0.6 multiply_reduce_fusion
  9.2 0.0 copy-start.4
  9.2 1.0 fusion.6
  10.3 7.7 %collective-permute-start = (bf16[2,512,104]{1,2,0:T(8,128)(2,1)S(1)}, bf16[2,512,104]{1,2,0:T(8,128)(2,1)S(1)}, u32[]{:S(2)}, u32[]{:S(2)}) collective-permute-start(bf16[2,512,104]{1,2,0:T(8,128)(2,1)S(1)} %slice.38), channel_id=1, source_target_pairs={{0,16},{16,0},{32,48},{48,32},{64,80},{80,64},{96,112},{112,96},{1... | collective-permute-start | bytes 638984 | tf_op jit(solution)/shard_map/ppermute | solution.py:12
  18.1 1.9 collective-permute-start.1
  20.0 3.6 %collective-permute-done.1 = s32[512]{0:T(512)S(1)} collective-permute-done((s32[512]{0:T(512)S(1)}, s32[512]{0:T(512)S(1)}, u32[]{:S(2)}, u32[]{:S(2)}) %collective-permute-start.1) | collective-permute-done | bytes 2080 | tf_op jit(solution)/shard_map/ppermute | solution.py:12
  23.6 0.0 collective-permute-done
  23.6 0.6 fusion.5
  24.2 1.4 copy-done.2
  25.5 0.7 fusion.13
  26.2 4.3 %fusion.4 = bf16[1664,512]{0,1:T(8,128)(2,1)} fusion(bf16[104,1664]{1,0:T(8,128)(2,1)S(1)} %copy-done.6, f32[512,1024]{1,0:T(8,128)} %copy-done.2, f32[512]{0:T(512)S(1)} %fusion.13, f32[512]{0:T(512)S(1)} %get-tuple-element.11, s32[1024]{0:T(1024)S(1)} %pad_add_fusion, s32[512]{0:T(512)S(1)} %copy-done.4, bf16[2,512,104]{1,2,0:T(8,128)(2,1)S(1)} %slice.38, ...), kind=kOutput, calls=%fused_computation.10 | convolution fusion | flops 290738176 | bytes 4583424 | tf_op jit(solution)/shard_map/dot_general | solution.py:62
  30.5 3.6 %copy.19 = bf16[1664,512]{1,0:T(8,128)(2,1)} copy(bf16[1664,512]{0,1:T(8,128)(2,1)} %fusion.4) | data formatting | bytes 3407872
  34.1 0.0 reduce-scatter.4.cloned.1.call-update
  34.1 0.0 all-gather.7.cloned.1.call-start
  34.2 2.0 convert_element_type.84
  36.2 60.3 %reduce-scatter.4.cloned.1.call-done = bf16[104,512]{1,0:T(8,128)(2,1)} async-done(((bf16[1664,512]{1,0:T(8,128)(2,1)}), bf16[104,512]{1,0:T(8,128)(2,1)}) %reduce-scatter.4.cloned.1.call-update) | async-done | bytes 106512
  96.5 1.0 copy.20
  97.5 1.2 fusion.49
  98.7 2.2 fusion.15
  100.9 0.0 all-gather.7.cloned.1.call-update
  100.9 0.0 copy-done.11
  100.9 0.1 fusion.64
  101.0 0.2 reduce_window_sum.30
  101.2 0.2 select_reduce_fusion.2
  101.4 0.1 select_reduce_fusion.1
  101.5 0.7 sub.80
  102.2 9.9 %all-to-all-start = ((s32[32,8,1]{1,2,0:T(1,128)}), s32[32,8,1]{1,2,0:T(1,128)S(1)}, u32[]{:S(2)}, u32[]{:S(2)}) async-start(s32[32,8,1]{1,2,0:T(1,128)} %bitcast), calls=%async_computation | async-start | bytes 32768 | tf_op jit(solution)/shard_map/all_to_all | solution.py:92
  112.1 32.5 %all-gather.7.cloned.1.call-done = bf16[2048,1024]{1,0:T(8,128)(2,1)} async-done(((bf16[128,1024]{1,0:T(8,128)(2,1)}), bf16[2048,1024]{1,0:T(8,128)(2,1)}) %all-gather.7.cloned.1.call-update) | async-done | bytes 4194320 | tf_op jit(solution)/shard_map/all_gather | solution.py:88
  144.6 3.1 reduce_sum.89
  147.7 0.0 copy-start.3
  147.7 1.1 fusion.14
  148.8 0.0 all-to-all-done
  148.8 9.8 %all-to-all-start.1 = ((bf16[32,8,1024]{2,1,0:T(8,128)(2,1)}), bf16[32,8,1024]{2,1,0:T(8,128)(2,1)S(1)}, u32[]{:S(2)}, u32[]{:S(2)}) async-start(bf16[32,8,1024]{2,1,0:T(8,128)(2,1)} %fusion.14), calls=%async_computation.1 | async-start | bytes 1048576 | tf_op jit(solution)/shard_map/all_to_all | solution.py:91
  158.7 0.0 all-gather.9.cloned.1.call-start
  158.8 0.1 sub.83
  158.9 0.1 compare_reduce_fusion
  158.9 0.1 ge.16
  159.0 0.2 fusion.45
  159.2 0.3 reduce-window.9
  159.5 0.1 slice.33
  159.6 0.1 slice_reduce_fusion
  159.7 0.1 fusion.65
  159.8 16.9 %all-to-all-done.1 = bf16[32,8,1024]{2,1,0:T(8,128)(2,1)S(1)} async-done(((bf16[32,8,1024]{2,1,0:T(8,128)(2,1)}), bf16[32,8,1024]{2,1,0:T(8,128)(2,1)S(1)}, u32[]{:S(2)}, u32[]{:S(2)}) %all-to-all-start.1) | async-done | bytes 524320 | tf_op jit(solution)/shard_map/all_to_all | solution.py:91
  176.7 0.4 fusion.42
  177.1 0.0 copy-start.5
  177.1 0.0 copy-start.9
  177.2 0.0 copy-start.10
  177.2 0.5 fusion.75
  177.7 0.3 multiply_reduce_fusion.1
  178.0 0.1 copy-done.5
  178.1 0.0 copy-done.9
  178.1 0.5 fusion.37
  178.7 0.6 fusion.74
  179.4 0.0 all-gather.9.cloned.1.call-update
  179.4 0.2 all-gather.11.cloned.1.call-start
  179.6 0.3 all-gather.11.cloned.1.call-update
  180.0 70.8 %all-gather.9.cloned.1.call-done = bf16[1,12288,64]{1,2,0:T(8,128)(2,1)} async-done(((bf16[1,384,64]{1,2,0:T(8,128)(2,1)}), bf16[1,12288,64]{1,2,0:T(8,128)(2,1)}) %all-gather.9.cloned.1.call-update) | async-done | bytes 1572880 | tf_op jit(solution)/shard_map/all_gather | solution.py:114
  250.7 9.3 %select_reduce_fusion = (f32[384]{0:T(512)S(1)}, f32[384,12288]{1,0:T(8,128)}) fusion(s32[384]{0:T(512)S(1)} %iota_add_fusion, bf16[1,12288,64]{1,2,0:T(8,128)(2,1)} %all-gather.9.cloned.1.call-done, bf16[3,384,64]{1,2,0:T(8,128)(2,1)S(1)} %convert_bitcast_fusion.1), kind=kOutput, calls=%fused_computation.1 | convolution fusion | flops 622853760 | bytes 20499968 | tf_op jit(solution)/shard_map/the,rhe->htr/dot_general | solution.py:117
  260.0 11.1 %fusion = f32[384]{0:T(512)S(1)} fusion(f32[384,12288]{1,0:T(8,128)} %get-tuple-element.16, f32[384]{0:T(512)S(1)} %broadcast_maximum_fusion, s32[384]{0:T(512)S(1)} %iota_add_fusion), kind=kLoop, calls=%fused_computation.4 | loop fusion | flops 18873984 | bytes 18878976 | tf_op jit(solution)/shard_map/reduce_sum | solution.py:123
  271.1 60.6 %all-gather.11.cloned.1.call-done = bf16[1,12288,64]{1,2,0:T(8,128)(2,1)} async-done(((bf16[1,384,64]{1,2,0:T(8,128)(2,1)}), bf16[1,12288,64]{1,2,0:T(8,128)(2,1)}) %all-gather.11.cloned.1.call-update) | async-done | bytes 1572880 | tf_op jit(solution)/shard_map/all_gather | solution.py:115
  331.8 11.1 %fusion.22 = bf16[384,64]{0,1:T(8,128)(2,1)} fusion(bf16[1,12288,64]{1,2,0:T(8,128)(2,1)} %all-gather.11.cloned.1.call-done, f32[384,12288]{1,0:T(8,128)} %get-tuple-element.16, f32[384]{0:T(512)S(1)} %broadcast_maximum_fusion, s32[384]{0:T(512)S(1)} %iota_add_fusion, f32[384]{0:T(512)S(1)} %fusion), kind=kOutput, calls=%fused_computation.34 | convolution fusion | flops 622903296 | bytes 20500992 | tf_op jit(solution)/shard_map/htr,rhe->hte/dot_general | solution.py:124
  (30 shorter events, 0.3 us)
Async XLA Ops:
  6.5 2.6 copy-start
  6.5 2.1 copy-start.1
  6.5 2.7 copy-start.8
  6.5 2.7 copy-start.7
  6.5 89.9 %reduce-scatter.4.cloned.1.call-start = ((), (), s32[]{:S(2)}) async-start(), calls=%async_computation.6 | async-start | bytes 1810432
  9.2 8.9 %copy-start.4 = (s32[512]{0:T(512)S(1)}, s32[512]{0:T(512)}, u32[]{:S(2)}) copy-start(s32[512]{0:T(512)} %param.13) | copy-start | bytes 6148
  10.3 13.2 %collective-permute-start = (bf16[2,512,104]{1,2,0:T(8,128)(2,1)S(1)}, bf16[2,512,104]{1,2,0:T(8,128)(2,1)S(1)}, u32[]{:S(2)}, u32[]{:S(2)}) collective-permute-start(bf16[2,512,104]{1,2,0:T(8,128)(2,1)S(1)} %slice.38), channel_id=1, source_target_pairs={{0,16},{16,0},{32,48},{48,32},{64,80},{80,64},{96,112},{112,96},{1... | collective-permute-start | bytes 638984 | tf_op jit(solution)/shard_map/ppermute | solution.py:12
  18.1 5.5 %collective-permute-start.1 = (s32[512]{0:T(512)S(1)}, s32[512]{0:T(512)S(1)}, u32[]{:S(2)}, u32[]{:S(2)}) collective-permute-start(s32[512]{0:T(512)S(1)} %copy-done.4), channel_id=1, source_target_pairs={{0,16},{16,0},{32,48},{48,32},{64,80},{80,64},{96,112},{112,96},{1... | collective-permute-start | bytes 6152 | tf_op jit(solution)/shard_map/ppermute | solution.py:12
  23.6 2.6 copy-start.6
  24.2 1.4 copy-start.2
  34.1 110.5 %all-gather.7.cloned.1.call-start = ((), (), s32[]{:S(2)}) async-start(), calls=%async_computation.3 | async-start | bytes 4456448 | tf_op jit(solution)/shard_map/all_gather | solution.py:88
  36.2 64.7 %copy-start.11 = (s32[128]{0:T(128)S(1)}, s32[128]{0:T(128)}, u32[]{:S(2)}) copy-start(s32[128]{0:T(128)} %param.19) | copy-start | bytes 1540
  102.2 46.6 %all-to-all-start = ((s32[32,8,1]{1,2,0:T(1,128)}), s32[32,8,1]{1,2,0:T(1,128)S(1)}, u32[]{:S(2)}, u32[]{:S(2)}) async-start(s32[32,8,1]{1,2,0:T(1,128)} %bitcast), calls=%async_computation | async-start | bytes 32768 | tf_op jit(solution)/shard_map/all_to_all | solution.py:92
  147.7 29.4 %copy-start.3 = (bf16[256,1024]{1,0:T(8,128)(2,1)S(1)}, bf16[256,1024]{1,0:T(8,128)(2,1)}, u32[]{:S(2)}) copy-start(bf16[256,1024]{1,0:T(8,128)(2,1)} %param.20) | copy-start | bytes 1572868
  148.8 27.9 %all-to-all-start.1 = ((bf16[32,8,1024]{2,1,0:T(8,128)(2,1)}), bf16[32,8,1024]{2,1,0:T(8,128)(2,1)S(1)}, u32[]{:S(2)}, u32[]{:S(2)}) async-start(bf16[32,8,1024]{2,1,0:T(8,128)(2,1)} %fusion.14), calls=%async_computation.1 | async-start | bytes 1048576 | tf_op jit(solution)/shard_map/all_to_all | solution.py:91
  158.7 92.1 %all-gather.9.cloned.1.call-start = ((), (), s32[]{:S(2)}) async-start(), calls=%async_computation.4 | async-start | bytes 1622016 | tf_op jit(solution)/shard_map/all_gather | solution.py:114
  177.1 1.0 copy-start.5
  177.1 1.0 copy-start.9
  177.2 1.0 copy-start.10
  179.4 152.4 %all-gather.11.cloned.1.call-start = ((), (), s32[]{:S(2)}) async-start(), calls=%async_computation.5 | async-start | bytes 1622016 | tf_op jit(solution)/shard_map/all_gather | solution.py:115
Sparse Core Ops, SparseCore 0:
  34.3 62.1 reduce-scatter.3
  101.0 43.5 all-gather.6
  179.5 71.1 all-gather.8
  254.2 77.5 all-gather.10
